TPU v7x, 32 devices: a whole 2x2x4 slice. The times are simulated.
32 devices in a mesh: tm: 16 (over z, x, core), doc: 2 (over y).
Axes of the slice: x: 2, y: 2, z: 4, core: 2. Of those that a mesh axis runs over, the one named last changes fastest.
Arguments:
- beta: float32 [16, 4096, 128], P('tm', 'doc'), may hold values from -6 to 260
- word_ids: int32 [16, 8, 128], P('tm', 'doc'), may hold values from 0 to 4095
- word_counts: int32 [16, 8, 128], P('tm', 'doc'), may hold values from 1 to 8
- block_slot: int32 [32], replicated, may hold values from 0 to 31, each once
- topic_prior: float32 [128], replicated, may hold values from 0.05 to 0.5
- drift_var: float32 [128], replicated, may hold values from 0.0005 to 0.05
- obs_precision: float32 [16, 128], replicated, may hold values from 0.01 to 4
Outputs:
- smoothed_means: float32 [16, 4096, 128], P('tm', 'doc')
- doc_topics: float32 [16, 8, 128], P('tm', 'doc')
Inputs may be any that keep to these rules, and one draw needn't show every extreme that they name: `block_slot`: each block has its own position.
All inputs are finite; a program needn't handle non-finite values.
Results may differ from a plain program's by a relative error of at most 0.0012.
The roundings to bfloat16 on the way count: a program that leaves them out, or rounds other values in their place, can miss the bound.
Values may be sent and summed in bfloat16 or wider, within the bound.
No kernel may reach another device: no remote copies, remote signals or barrier semaphores. Data moves between devices by JAX's collectives and lax.ppermute only.
A program may use at most 192 MiB of HBM per device.

v0:
```python
import jax
import jax.numpy as jnp
from jax import lax
from jax.sharding import PartitionSpec as P

K = 128
BLOCK = 128
EITERS = 4
init_variance = 4.0


def variance_tables(obs_precision, drift_var):

    def forward_step(prior_var, precision):
        denominator = 1.0 + prior_var * precision
        gain_now = prior_var * precision / denominator
        filt_var = prior_var / denominator
        return (filt_var + drift_var, (gain_now, filt_var))

    start_var = jnp.full(drift_var.shape, init_variance, dtype=jnp.float32)
    last_var, (gains, filt_vars) = lax.scan(forward_step, start_var, obs_precision)

    def backward_step(info_next, precision):
        merged = info_next + precision
        shrink = 1.0 / (1.0 + drift_var * merged)
        info_now = merged * shrink
        return (info_now, (shrink, info_now))

    zero_info = jnp.zeros(drift_var.shape, dtype=jnp.float32)
    last_info, (shrinks, infos) = lax.scan(
        backward_step, zero_info, obs_precision[1:], reverse=True
    )
    shrinks = jnp.concatenate([shrinks, jnp.ones_like(zero_info)[None]], axis=0)
    infos = jnp.concatenate([infos, zero_info[None]], axis=0)
    return (gains, filt_vars, shrinks, infos)


def e_step(looked, word_counts, topic_prior):
    counts_float = word_counts.astype(jnp.float32)
    doc_topics = topic_prior + jnp.sum(counts_float, axis=-1, keepdims=True) / K
    scores = looked.astype(jnp.float32)
    for sweep in range(EITERS):
        resp = jax.nn.softmax(lax.digamma(doc_topics)[..., None, :] + scores, axis=-1)
        doc_topics = topic_prior + jnp.sum(counts_float[..., None] * resp, axis=-2)
    weighted = (counts_float[..., None] * resp).astype(jnp.bfloat16)
    return (doc_topics, weighted)


def body(beta, word_ids, word_counts, block_slot, topic_prior, drift_var, obs_precision):
    local_beta = beta[0]
    own_words = local_beta.shape[0]
    topics = local_beta.shape[1]
    doc_devices = lax.axis_size("doc")
    doc_place = lax.axis_index("doc")
    local_peak = jnp.max(local_beta, axis=0)
    local_total = jnp.sum(jnp.exp(local_beta - local_peak), axis=0)
    slot_ids = word_ids[0]
    local_docs = slot_ids.shape[0]
    slot_width = slot_ids.shape[1]
    columns = jnp.take(block_slot, slot_ids // BLOCK) * BLOCK + slot_ids % BLOCK
    all_columns = lax.all_gather(columns, "doc", axis=0, tiled=True)
    all_counts = lax.all_gather(word_counts[0], "doc", axis=0, tiled=True)
    peaks = lax.all_gather(local_peak, "doc")
    totals = lax.all_gather(local_total, "doc")
    peak_value = jnp.max(peaks, axis=0)
    total_value = jnp.sum(totals * jnp.exp(peaks - peak_value), axis=0)
    normalizer = peak_value + jnp.log(total_value)
    flat_columns = all_columns.reshape(-1)
    local_columns = flat_columns - doc_place * own_words
    inside = (local_columns >= 0) & (local_columns < own_words)
    picked = jnp.take(local_beta, jnp.clip(local_columns, 0, own_words - 1), axis=0)
    partial = jnp.where(
        inside[:, None], (picked - normalizer).astype(jnp.bfloat16), jnp.zeros((), jnp.bfloat16)
    )
    looked = lax.psum(partial, "doc").reshape(local_docs * doc_devices, slot_width, topics)
    doc_topics_all, weighted = e_step(looked, all_counts, topic_prior)
    doc_topics = lax.dynamic_slice_in_dim(doc_topics_all, doc_place * local_docs, local_docs, 0)
    flat_weighted = weighted.reshape(-1, topics)
    row_words = lax.iota(jnp.int32, own_words)
    marks = (row_words[:, None] == local_columns[None, :]).astype(jnp.bfloat16)
    counts = jnp.dot(marks, flat_weighted, preferred_element_type=jnp.float32)
    pseudo = local_beta + jnp.log1p(counts)
    gains, filt_vars, shrinks, infos = variance_tables(obs_precision, drift_var)
    years_total = obs_precision.shape[0]
    pulls = filt_vars / (filt_vars + drift_var)
    pulls = pulls.at[-1].set(0.0)
    years = lax.axis_size("tm")
    chunk = own_words // years
    by_year = lax.all_to_all(
        pseudo.reshape(years, chunk, topics), "tm", split_axis=0, concat_axis=0, tiled=True
    )

    def filter_step(mean_prev, inputs):
        gain_now, pseudo_now = inputs
        mean_now = (1.0 - gain_now) * mean_prev + gain_now * pseudo_now
        return (mean_now, mean_now)

    zero_mean = jnp.zeros((chunk, topics), dtype=jnp.float32)
    last_mean, filtered = lax.scan(
        filter_step, zero_mean, (gains[:, None, :], by_year), unroll=True
    )

    def smooth_step(mean_next, inputs):
        pull_now, filt_now = inputs
        mean_now = pull_now * mean_next + (1.0 - pull_now) * filt_now
        return (mean_now, mean_now)

    first_mean, smoothed = lax.scan(
        smooth_step, zero_mean, (pulls[:, None, :], filtered), reverse=True, unroll=True
    )
    back = lax.all_to_all(smoothed, "tm", split_axis=0, concat_axis=0, tiled=True)
    return (back.reshape(own_words, topics)[None], doc_topics[None])


def solution(mesh):
    in_specs = (
        P("tm", "doc", None),
        P("tm", "doc", None),
        P("tm", "doc", None),
        P(),
        P(),
        P(),
        P(),
    )
    out_specs = (P("tm", "doc", None), P("tm", "doc", None))
    return jax.shard_map(body, mesh=mesh, in_specs=in_specs, out_specs=out_specs, check_vma=False)
```

profile of v0, /device:TPU:9, one launch (start us, length us, event | category | flops | bytes accessed | tf_op | source)
XLA Modules:
  0.0 144.6 jit_solution(16217126004983186146)
XLA Ops:
  7.2 1.6 %reduce_max.54 = f32[128]{0:T(128)S(1)} reduce(f32[1,2048,128]{2,1,0:T(8,128)} %param.11, f32[]{:T(128)} %constant.154.clone.1), dimensions={0,1}, to_apply=%region_3.4 | reduce | flops 262016 | bytes 1049092 | tf_op jit(solution)/shard_map/reduce_max | solution.py:55
  9.1 3.1 %all-gather.5 = f32[2,1,128]{2,1,0:T(1,128)S(1)} all-gather(f32[1,1,128]{2,1,0:T(1,128)S(1)} %bitcast.281), channel_id=4, replica_groups=mesh['tm'=16,'doc'=2] {'doc'}, dimensions={0}, use_global_device_ids=true | all-gather | bytes 1536 | tf_op jit(solution)/shard_map/all_gather | solution.py:64
  12.2 3.1 %all-gather.4 = f32[2,1,128]{2,1,0:T(1,128)S(1)} all-gather(f32[1,1,128]{2,1,0:T(1,128)S(1)} %bitcast.278), channel_id=3, replica_groups=mesh['tm'=16,'doc'=2] {'doc'}, dimensions={0}, use_global_device_ids=true | all-gather | bytes 1536 | tf_op jit(solution)/shard_map/all_gather | solution.py:63
  15.4 3.3 %gather_fusion = s32[512]{0:T(512)S(1)} fusion(s32[32]{0:T(128)S(1)} %copy-done, s32[1024]{0:T(1024)S(1)} %pad_clamp_fusion), kind=kCustom, calls=%fused_computation | custom fusion | bytes 6144 | tf_op jit(solution)/shard_map/jit(_take)/gather | solution.py:60
  18.8 3.2 %all-gather.3 = s32[2,4,128]{2,1,0:T(4,128)S(1)} all-gather(s32[1,4,128]{2,1,0:T(4,128)S(1)} %fusion.120), channel_id=1, replica_groups=mesh['tm'=16,'doc'=2] {'doc'}, dimensions={0}, use_global_device_ids=true | all-gather | bytes 6144 | tf_op jit(solution)/shard_map/all_gather | solution.py:61
  22.0 2.8 %gather_fusion.1 = f32[1024,128]{1,0:T(8,128)S(1)} fusion(f32[2048,128]{1,0:T(8,128)S(1)} %bitcast.257, s32[1024]{0:T(1024)S(1)} %broadcast_clamp_fusion), kind=kCustom, calls=%fused_computation.1 | custom fusion | bytes 1052672 | tf_op jit(solution)/shard_map/jit(_take)/gather | solution.py:71
  24.9 1.0 fusion.24
  25.9 3.2 %all-gather = s32[1,8,128]{2,0,1:T(1,128)S(1)} all-gather(s32[1,4,128]{2,0,1:T(1,128)S(1)} %bitcast.279), channel_id=2, replica_groups=mesh['tm'=16,'doc'=2] {'doc'}, dimensions={1}, use_global_device_ids=true | all-gather | bytes 6144 | tf_op jit(solution)/shard_map/all_gather | solution.py:62
  29.5 24.0 %all-reduce.2.cloned.1.call-done = bf16[1024,128]{1,0:T(8,128)(2,1)} async-done(((bf16[1024,128]{1,0:T(8,128)(2,1)}), bf16[1024,128]{1,0:T(8,128)(2,1)}) %all-reduce.2.cloned.1.call-update) | async-done | bytes 262160 | tf_op jit(solution)/shard_map/psum | solution.py:75
  53.5 1.2 fusion.6
  54.7 1.3 fusion.23
  56.1 1.4 multiply_reduce_fusion.3
  57.5 1.2 fusion.8
  61.9 2.8 %fusion.4 = f32[2048,128]{1,0:T(8,128)} fusion(bf16[1024,128]{1,0:T(8,128)(2,1)S(1)} %fusion.17, s32[1024]{0:T(1024)S(1)} %bitcast.274, f32[1,2048,128]{2,1,0:T(8,128)S(1)} %copy-done.2), kind=kOutput, calls=%fused_computation.11 | convolution fusion | flops 539230208 | bytes 2363392 | tf_op jit(solution)/shard_map/dot_general | solution.py:81
  64.7 7.0 %all-to-all-start = ((f32[16,128,128]{2,1,0:T(8,128)}), f32[16,128,128]{2,1,0:T(8,128)S(1)}, u32[]{:S(2)}, u32[]{:S(2)}) async-start(f32[16,128,128]{2,1,0:T(8,128)} %bitcast.59), calls=%async_computation | async-start | bytes 2097152 | tf_op jit(solution)/shard_map/all_to_all | solution.py:89
  71.7 12.5 %while.16 = (s32[]{:T(128)}, f32[128]{0:T(128)S(1)}, f32[16,128]{1,0:T(8,128)S(1)}, f32[16,128]{1,0:T(8,128)S(1)}, f32[16,128]{1,0:T(8,128)}, /*index=5*/f32[128]{0:T(128)S(1)}, s32[]{:T(128)}, s32[]{:T(128)}) while((s32[]{:T(128)}, f32[128]{0:T(128)S(1)}, f32[16,128]{1,0:T(8,128)S(1)}, f32[16,128]{1,0:T(8,128)S(1)}, ...), condition=%wide.region_1.0_spmd.clone, body=%wide.region_0.0_spmd.clone.sunk | while | flops 771 | bytes 5235 | solution.py:21
  71.7 0.7 fusion.137
  72.5 0.7 fusion.137
  73.3 0.7 fusion.137
  84.3 12.3 %all-to-all-done = f32[16,128,128]{2,1,0:T(8,128)S(1)} async-done(((f32[16,128,128]{2,1,0:T(8,128)}), f32[16,128,128]{2,1,0:T(8,128)S(1)}, u32[]{:S(2)}, u32[]{:S(2)}) %all-to-all-start) | async-done | bytes 1048608 | tf_op jit(solution)/shard_map/all_to_all | solution.py:89
  96.6 0.9 add_dynamic-update-slice_fusion
  107.1 4.8 %all-to-all-start.1 = ((f32[16,128,128]{2,1,0:T(8,128)}), f32[16,128,128]{2,1,0:T(8,128)S(1)}, u32[]{:S(2)}, u32[]{:S(2)}) async-start(f32[16,128,128]{2,1,0:T(8,128)} %fusion.41), calls=%async_computation.1 | async-start | bytes 2097152 | tf_op jit(solution)/shard_map/all_to_all | solution.py:111
  113.0 23.8 %all-to-all-done.1 = f32[16,128,128]{2,1,0:T(8,128)S(1)} async-done(((f32[16,128,128]{2,1,0:T(8,128)}), f32[16,128,128]{2,1,0:T(8,128)S(1)}, u32[]{:S(2)}, u32[]{:S(2)}) %all-to-all-start.1) | async-done | bytes 1048608 | tf_op jit(solution)/shard_map/all_to_all | solution.py:111
  136.8 1.0 copy.43
  (113 shorter events, 24.8 us)
Async XLA Ops:
  7.2 8.2 %copy-start = (s32[32]{0:T(128)S(1)}, s32[32]{0:T(128)}, u32[]{:S(2)}) copy-start(s32[32]{0:T(128)} %param.14) | copy-start | bytes 388
  7.2 1.7 %copy-start.2 = (f32[1,2048,128]{2,1,0:T(8,128)S(1)}, f32[1,2048,128]{2,1,0:T(8,128)}, u32[]{:S(2)}) copy-start(f32[1,2048,128]{2,1,0:T(8,128)} %param.11) | copy-start | bytes 3145732
  7.2 46.3 %all-reduce.2.cloned.1.call-start = ((), (), s32[]{:S(2)}) async-start(), calls=%async_computation.2 | async-start | bytes 524288 | tf_op jit(solution)/shard_map/psum | solution.py:75
  7.2 8.1 %copy-start.5 = (s32[1,4,128]{2,1,0:T(4,128)S(1)}, s32[1,4,128]{2,1,0:T(4,128)}, u32[]{:S(2)}) copy-start(s32[1,4,128]{2,1,0:T(4,128)} %param.12) | copy-start | bytes 6148
  24.8 1.1 copy-start.6
  24.8 4.5 %copy-start.4 = (f32[128]{0:T(128)S(1)}, f32[128]{0:T(128)}, u32[]{:S(2)}) copy-start(f32[128]{0:T(128)} %param.15) | copy-start | bytes 1540
  53.5 5.2 %copy-start.1 = (bf16[1024,128]{1,0:T(8,128)(2,1)S(1)}, bf16[1024,128]{1,0:T(8,128)(2,1)}, u32[]{:S(2)}) copy-start(bf16[1024,128]{1,0:T(8,128)(2,1)} %all-reduce.2.cloned.1.call-done) | copy-start | bytes 786436
  64.7 7.0 %copy-start.3 = (f32[128]{0:T(128)S(1)}, f32[128]{0:T(128)}, u32[]{:S(2)}) copy-start(f32[128]{0:T(128)} %param.16) | copy-start | bytes 1540
  64.7 31.9 %all-to-all-start = ((f32[16,128,128]{2,1,0:T(8,128)}), f32[16,128,128]{2,1,0:T(8,128)S(1)}, u32[]{:S(2)}, u32[]{:S(2)}) async-start(f32[16,128,128]{2,1,0:T(8,128)} %bitcast.59), calls=%async_computation | async-start | bytes 2097152 | tf_op jit(solution)/shard_map/all_to_all | solution.py:89
  107.1 29.7 %all-to-all-start.1 = ((f32[16,128,128]{2,1,0:T(8,128)}), f32[16,128,128]{2,1,0:T(8,128)S(1)}, u32[]{:S(2)}, u32[]{:S(2)}) async-start(f32[16,128,128]{2,1,0:T(8,128)} %fusion.41), calls=%async_computation.1 | async-start | bytes 2097152 | tf_op jit(solution)/shard_map/all_to_all | solution.py:111
Sparse Core Ops, SparseCore 0:
  26.0 27.4 all-reduce.1
where the time goes:
time: 146 us; the launch traced here: 145 us
  waiting for transfers between devices  60.2 us (41%)
  other arithmetic  29.6 us (20%)
  between operations  14.3 us (10%)
  local copies, waits for them, and re-layouts  13.1 us (9%)
  blocking collectives  12.6 us (9%)
  starting transfers between devices  11.8 us (8%)
  matrix products  2.76 us (2%)
    psum x1, waiting for transfers between devices, body(): lax.psum(partial, 'doc')  24 us
    all_to_all x1, waiting for transfers between devices, body(): lax.all_to_all(smoothed, 'tm', split_axis=0, concat_axis=0, tiled=True)  23.8 us
    all_to_all x1, waiting for transfers between devices, body(): lax.all_to_all(pseudo.reshape(years, chunk, topics), 'tm', split_axis=0,...  12.3 us
    add x16, other arithmetic, forward_step(): return (filt_var + drift_var, (gain_now, filt_var))  11.4 us
    all_to_all x1, starting transfers between devices, body(): lax.all_to_all(pseudo.reshape(years, chunk, topics), 'tm', split_axis=0,...  6.99 us
    unnamed x22, local copies, waits for them, and re-layouts  5.44 us
    unnamed x10, other arithmetic  5.43 us
    all_to_all x1, starting transfers between devices, body(): lax.all_to_all(smoothed, 'tm', split_axis=0, concat_axis=0, tiled=True)  4.76 us
  transfers between devices with their start and end apart: 3, of which 3 were waited for; matrix products, arithmetic and copies ran while one was open for 9% of the time, Pallas kernels for 0%

commit v1 on v0

--- a/solution.py
+++ b/solution.py
@@ -7,6 +7,10 @@
 BLOCK = 128
 EITERS = 4
 init_variance = 4.0
+
+
+def samples_list(view, mesh_name):
+    return jnp.sum(lax.all_gather(view, axis_name=mesh_name), 0)
 
 
 def variance_tables(obs_precision, drift_var):
@@ -72,7 +76,7 @@
     partial = jnp.where(
         inside[:, None], (picked - normalizer).astype(jnp.bfloat16), jnp.zeros((), jnp.bfloat16)
     )
-    looked = lax.psum(partial, "doc").reshape(local_docs * doc_devices, slot_width, topics)
+    looked = samples_list(partial, "doc").reshape(local_docs * doc_devices, slot_width, topics)
     doc_topics_all, weighted = e_step(looked, all_counts, topic_prior)
     doc_topics = lax.dynamic_slice_in_dim(doc_topics_all, doc_place * local_docs, local_docs, 0)
     flat_weighted = weighted.reshape(-1, topics)

time: 146 us -> 118 us (0.81)
  waiting for transfers between devices: 60.2 us -> 36.1 us
  between operations: 14.3 us -> 0.92 us
  blocking collectives: 12.6 us -> 18.7 us
  starting transfers between devices: 11.8 us -> 17.2 us
  other arithmetic: 29.6 us -> 27.8 us
    psum x1 -> x0, waiting for transfers between devices: 24 us -> none  [body(): lax.psum(partial, 'doc')]
    all_gather x0 -> x1, blocking collectives: none -> 5.89 us  [samples_list(): return jnp.sum(lax.all_gather(view, axis_name=mesh_name), 0)]
    div x0 -> x3, other arithmetic: none -> 5.83 us  [e_step(): jax.nn.softmax(lax.digamma(doc_topics)[..., None, :] + scores, axis=-1)]
    all_to_all x1, starting transfers between devices: 6.99 us -> 12.4 us  [body(): lax.all_to_all(pseudo.reshape(years, chunk, topics), 'tm', split_axis=0,...]
    reduce_max x4 -> x1, other arithmetic: 2.83 us -> 0.22 us  [e_step(): jax.nn.softmax(lax.digamma(doc_topics)[..., None, :] + scores, axis=-1)]
    reduce_sum x4 -> x1, other arithmetic: 2.88 us -> 0.48 us  [e_step(): doc_topics = topic_prior + jnp.sum(counts_float[..., None] * resp, axis=-2)]
    reduce_sum x4 -> x1, other arithmetic: 2.48 us -> 0.39 us  [e_step(): jax.nn.softmax(lax.digamma(doc_topics)[..., None, :] + scores, axis=-1)]
    unnamed x22 -> x18, local copies, waits for them, and re-layouts: 5.44 us -> 5.44 us
  transfers between devices with their start and end apart: 3 -> 2, of which waited for: 3 -> 2; matrix products, arithmetic and copies ran while one was open for 9% -> 11% of each run, Pallas kernels for 0% -> 0%
where the time goes in v1:
time: 118 us; the launch traced here: 117 us
  waiting for transfers between devices  36.1 us (31%)
  other arithmetic  27.8 us (24%)
  blocking collectives  18.7 us (16%)
  starting transfers between devices  17.2 us (15%)
  local copies, waits for them, and re-layouts  13.1 us (11%)
  matrix products  2.76 us (2%)
    all_to_all x1, waiting for transfers between devices, body(): lax.all_to_all(smoothed, 'tm', split_axis=0, concat_axis=0, tiled=True)  23.8 us
    all_to_all x1, starting transfers between devices, body(): lax.all_to_all(pseudo.reshape(years, chunk, topics), 'tm', split_axis=0,...  12.4 us
    all_to_all x1, waiting for transfers between devices, body(): lax.all_to_all(pseudo.reshape(years, chunk, topics), 'tm', split_axis=0,...  12.3 us
    add x16, other arithmetic, forward_step(): return (filt_var + drift_var, (gain_now, filt_var))  11.3 us
    all_gather x1, blocking collectives, samples_list(): return jnp.sum(lax.all_gather(view, axis_name=mesh_name), 0)  5.89 us
    div x3, other arithmetic, e_step(): jax.nn.softmax(lax.digamma(doc_topics)[..., None, :] + scores, axis=-1)  5.83 us
    unnamed x18, local copies, waits for them, and re-layouts  5.44 us
    unnamed x10, other arithmetic  5.43 us
  transfers between devices with their start and end apart: 2, of which 2 were waited for; matrix products, arithmetic and copies ran while one was open for 11% of the time, Pallas kernels for 0%

profile of v1, /device:TPU:9, one launch (start us, length us, event | category | flops | bytes accessed | tf_op | source)
XLA Modules:
  0.0 116.9 jit_solution(3678050226903893093)
XLA Ops:
  0.7 3.5 %all-gather = s32[1,8,128]{2,0,1:T(1,128)S(1)} all-gather(s32[1,4,128]{2,0,1:T(1,128)} %bitcast.243), channel_id=2, replica_groups=mesh['tm'=16,'doc'=2] {'doc'}, dimensions={1}, use_global_device_ids=true | all-gather | bytes 6144 | tf_op jit(solution)/shard_map/all_gather | solution.py:66
  4.3 1.5 %reduce_max.56 = f32[128]{0:T(128)S(1)} reduce(f32[1,2048,128]{2,1,0:T(8,128)} %param.11, f32[]{:T(128)} %constant.155.clone.1), dimensions={0,1}, to_apply=%region_3.4 | reduce | flops 262016 | bytes 1049092 | tf_op jit(solution)/shard_map/reduce_max | solution.py:59
  6.1 3.1 %all-gather.5 = f32[2,1,128]{2,1,0:T(1,128)S(1)} all-gather(f32[1,1,128]{2,1,0:T(1,128)S(1)} %bitcast.245), channel_id=4, replica_groups=mesh['tm'=16,'doc'=2] {'doc'}, dimensions={0}, use_global_device_ids=true | all-gather | bytes 1536 | tf_op jit(solution)/shard_map/all_gather | solution.py:68
  9.2 3.1 %all-gather.4 = f32[2,1,128]{2,1,0:T(1,128)S(1)} all-gather(f32[1,1,128]{2,1,0:T(1,128)S(1)} %bitcast.242), channel_id=3, replica_groups=mesh['tm'=16,'doc'=2] {'doc'}, dimensions={0}, use_global_device_ids=true | all-gather | bytes 1536 | tf_op jit(solution)/shard_map/all_gather | solution.py:67
  12.4 3.3 %gather_fusion = s32[512]{0:T(512)S(1)} fusion(s32[32]{0:T(128)S(1)} %copy-done, s32[1024]{0:T(1024)S(1)} %pad_clamp_fusion), kind=kCustom, calls=%fused_computation | custom fusion | bytes 6144 | tf_op jit(solution)/shard_map/jit(_take)/gather | solution.py:64
  15.7 3.2 %all-gather.3 = s32[2,4,128]{2,1,0:T(4,128)S(1)} all-gather(s32[1,4,128]{2,1,0:T(4,128)S(1)} %fusion.139), channel_id=1, replica_groups=mesh['tm'=16,'doc'=2] {'doc'}, dimensions={0}, use_global_device_ids=true | all-gather | bytes 6144 | tf_op jit(solution)/shard_map/all_gather | solution.py:65
  19.0 2.8 %gather_fusion.1 = f32[1024,128]{1,0:T(8,128)S(1)} fusion(f32[2048,128]{1,0:T(8,128)S(1)} %bitcast.222, s32[1024]{0:T(1024)S(1)} %broadcast_clamp_fusion), kind=kCustom, calls=%fused_computation.1 | custom fusion | bytes 1052672 | tf_op jit(solution)/shard_map/jit(_take)/gather | solution.py:75
  22.2 5.9 %all_gather.28 = bf16[2,1024,128]{2,1,0:T(8,128)(2,1)S(1)} all-gather(bf16[1,1024,128]{2,1,0:T(8,128)(2,1)S(1)} %fusion.34), channel_id=1, replica_groups=mesh['tm'=16,'doc'=2] {'doc'}, dimensions={0}, use_global_device_ids=true | all-gather | bytes 786432 | tf_op jit(solution)/shard_map/all_gather | solution.py:13
  28.5 1.9 %fusion.157 = f32[8,128]{1,0:T(8,128)S(1)} fusion(f32[8,128,128]{2,1,0:T(8,128)S(1)} %bitcast.223, f32[8,128]{1,0:T(8,128)S(1)} %fusion.63, f32[8,128]{1,0:T(8,128)S(1)} %bitcast.232), kind=kOutput, calls=%fused_computation.314 | output fusion | flops 656638 | bytes 536576 | tf_op jit(solution)/shard_map/div | solution.py:47
  30.5 1.9 %fusion.160 = f32[8,128]{1,0:T(8,128)S(1)} fusion(f32[8,128,128]{2,1,0:T(8,128)S(1)} %bitcast.224, f32[8,128]{1,0:T(8,128)S(1)} %fusion.65, f32[8,128]{1,0:T(8,128)S(1)} %bitcast.233), kind=kOutput, calls=%fused_computation.315 | output fusion | flops 656638 | bytes 536576 | tf_op jit(solution)/shard_map/div | solution.py:47
  32.5 1.9 %fusion.163 = f32[8,128]{1,0:T(8,128)S(1)} fusion(f32[8,128,128]{2,1,0:T(8,128)S(1)} %bitcast.225, f32[8,128]{1,0:T(8,128)S(1)} %fusion.67, f32[8,128]{1,0:T(8,128)S(1)} %bitcast.234), kind=kOutput, calls=%fused_computation.316 | output fusion | flops 656638 | bytes 536576 | tf_op jit(solution)/shard_map/div | solution.py:47
  35.6 2.8 %fusion.10 = f32[2048,128]{1,0:T(8,128)} fusion(bf16[1024,128]{1,0:T(8,128)(2,1)S(1)} %fusion.29, s32[1024]{0:T(1024)S(1)} %bitcast.238, f32[1,2048,128]{2,1,0:T(8,128)S(1)} %copy-done.1), kind=kOutput, calls=%fused_computation.17 | convolution fusion | flops 539230208 | bytes 2363392 | tf_op jit(solution)/shard_map/dot_general | solution.py:85
  38.3 12.4 %all-to-all-start = ((f32[16,128,128]{2,1,0:T(8,128)}), f32[16,128,128]{2,1,0:T(8,128)S(1)}, u32[]{:S(2)}, u32[]{:S(2)}) async-start(f32[16,128,128]{2,1,0:T(8,128)} %bitcast.53), calls=%async_computation | async-start | bytes 2097152 | tf_op jit(solution)/shard_map/all_to_all | solution.py:93
  50.8 12.5 %while.16 = (s32[]{:T(128)}, f32[128]{0:T(128)S(1)}, f32[16,128]{1,0:T(8,128)S(1)}, f32[16,128]{1,0:T(8,128)S(1)}, f32[16,128]{1,0:T(8,128)}, /*index=5*/f32[128]{0:T(128)S(1)}, s32[]{:T(128)}, s32[]{:T(128)}) while((s32[]{:T(128)}, f32[128]{0:T(128)S(1)}, f32[16,128]{1,0:T(8,128)S(1)}, f32[16,128]{1,0:T(8,128)S(1)}, ...), condition=%wide.region_1.0_spmd.clone, body=%wide.region_0.0_spmd.clone.sunk | while | flops 771 | bytes 5235 | solution.py:25
  51.6 0.7 fusion.168
  52.4 0.7 fusion.168
  54.0 0.7 fusion.168
  54.7 0.7 fusion.168
  56.3 0.7 fusion.168
  63.4 12.3 %all-to-all-done = f32[16,128,128]{2,1,0:T(8,128)S(1)} async-done(((f32[16,128,128]{2,1,0:T(8,128)}), f32[16,128,128]{2,1,0:T(8,128)S(1)}, u32[]{:S(2)}, u32[]{:S(2)}) %all-to-all-start) | async-done | bytes 1048608 | tf_op jit(solution)/shard_map/all_to_all | solution.py:93
  75.7 0.9 add_dynamic-update-slice_fusion
  86.2 4.8 %all-to-all-start.1 = ((f32[16,128,128]{2,1,0:T(8,128)}), f32[16,128,128]{2,1,0:T(8,128)S(1)}, u32[]{:S(2)}, u32[]{:S(2)}) async-start(f32[16,128,128]{2,1,0:T(8,128)} %fusion.60), calls=%async_computation.1 | async-start | bytes 2097152 | tf_op jit(solution)/shard_map/all_to_all | solution.py:115
  92.1 23.8 %all-to-all-done.1 = f32[16,128,128]{2,1,0:T(8,128)S(1)} async-done(((f32[16,128,128]{2,1,0:T(8,128)}), f32[16,128,128]{2,1,0:T(8,128)S(1)}, u32[]{:S(2)}, u32[]{:S(2)}) %all-to-all-start.1) | async-done | bytes 1048608 | tf_op jit(solution)/shard_map/all_to_all | solution.py:115
  115.9 1.0 copy.43
  (103 shorter events, 21.9 us)
Async XLA Ops:
  0.6 11.7 %copy-start = (s32[32]{0:T(128)S(1)}, s32[32]{0:T(128)}, u32[]{:S(2)}) copy-start(s32[32]{0:T(128)} %param.14) | copy-start | bytes 388
  0.6 5.2 %copy-start.1 = (f32[1,2048,128]{2,1,0:T(8,128)S(1)}, f32[1,2048,128]{2,1,0:T(8,128)}, u32[]{:S(2)}) copy-start(f32[1,2048,128]{2,1,0:T(8,128)} %param.11) | copy-start | bytes 3145732
  4.3 8.0 %copy-start.4 = (s32[1,4,128]{2,1,0:T(4,128)S(1)}, s32[1,4,128]{2,1,0:T(4,128)}, u32[]{:S(2)}) copy-start(s32[1,4,128]{2,1,0:T(4,128)} %param.12) | copy-start | bytes 6148
  22.2 6.1 %copy-start.3 = (f32[128]{0:T(128)S(1)}, f32[128]{0:T(128)}, u32[]{:S(2)}) copy-start(f32[128]{0:T(128)} %param.15) | copy-start | bytes 1540
  38.3 12.5 %copy-start.2 = (f32[128]{0:T(128)S(1)}, f32[128]{0:T(128)}, u32[]{:S(2)}) copy-start(f32[128]{0:T(128)} %param.16) | copy-start | bytes 1540
  38.3 37.4 %all-to-all-start = ((f32[16,128,128]{2,1,0:T(8,128)}), f32[16,128,128]{2,1,0:T(8,128)S(1)}, u32[]{:S(2)}, u32[]{:S(2)}) async-start(f32[16,128,128]{2,1,0:T(8,128)} %bitcast.53), calls=%async_computation | async-start | bytes 2097152 | tf_op jit(solution)/shard_map/all_to_all | solution.py:93
  86.2 29.7 %all-to-all-start.1 = ((f32[16,128,128]{2,1,0:T(8,128)}), f32[16,128,128]{2,1,0:T(8,128)S(1)}, u32[]{:S(2)}, u32[]{:S(2)}) async-start(f32[16,128,128]{2,1,0:T(8,128)} %fusion.60), calls=%async_computation.1 | async-start | bytes 2097152 | tf_op jit(solution)/shard_map/all_to_all | solution.py:115
